TPU v7x, 256 devices: a whole 4x4x8 slice. The times are simulated.
256 devices in a mesh: group: 8 (over x, core), inner: 32 (over z, y).
Axes of the slice: x: 4, y: 4, z: 8, core: 2. Of those that a mesh axis runs over, the one named last changes fastest.
Arguments:
- flow_field: float32 [1536, 1536, 128], P('inner', 'group'), may hold values from -6 to 6
- sketch_rows: float32 [1536, 128], P('inner'), may hold values from -6 to 6
- sketch_cols: float32 [1536, 128], P('group'), may hold values from -6 to 6
- sketch_depth: float32 [128, 128], replicated, may hold values from -6 to 6
- bit_widths: int32 [2], replicated, may hold values from 6 to 8
- bin_edges: int32 [9], replicated, may hold values from -6 to 6, as said below
Outputs:
- basis_one: float32 [1536, 128], P('inner')
- basis_two: float32 [1536, 128], P('group')
- core: float32 [128, 128, 128], P('inner', 'group')
- residual: float32 [2, 128, 128, 128], P(None, 'inner', 'group')
- energy: float32 [2, 1536, 128], P(None, 'inner')
- histogram: float32 [2, 1536, 8], P(None, 'inner')
Inputs may be any that keep to these rules, and one draw needn't show every extreme that they name: `bin_edges`: strictly increasing; the first is -6 and the last 6.
All inputs are finite; a program needn't handle non-finite values.
Results may differ from a plain program's by a relative error of at most 0.0008.
Values sent between devices are 32-bit elements; how exact they have to be, the bound alone decides.
No kernel may reach another device: no remote copies, remote signals or barrier semaphores. Data moves between devices by JAX's collectives and lax.ppermute only.
A program may use at most 128 MiB of HBM per device.

v0:
```python
import math
import jax
import jax.numpy as jnp
from jax import lax
from jax.sharding import PartitionSpec as P

N1 = 1536
N2 = 1536
N3 = 128
R = 128
NEDGE = 9
NBINS = 8
precise = lax.Precision.HIGHEST
two_pi = 2.0 * 3.141592653589793
error_boost = 16.0


def gram_of(sketch):
    return jnp.dot(sketch.T, sketch, precision=precise)


def orthonormal_rows(sketch, gram_matrix):
    lower_factor = jnp.linalg.cholesky(gram_matrix)
    return jax.scipy.linalg.solve_triangular(lower_factor, sketch.T, lower=True).T


def soft_residual(core_values, step_size):
    return -jnp.sin(two_pi * core_values[None] / step_size[:, None, None, None]) / two_pi


def local(flow_field, sketch_rows, sketch_cols, sketch_depth, bit_widths, bin_edges):
    reduced = jnp.einsum("ijk,kr->ijr", flow_field, sketch_depth, precision=precise)
    mode_one = jnp.einsum("ijr,jr->ir", reduced, sketch_cols, precision=precise)
    mode_two = jnp.einsum("ijr,ir->jr", reduced, sketch_rows, precision=precise)
    mode_one = lax.psum(mode_one, "group")
    basis_one = orthonormal_rows(mode_one, lax.psum(gram_of(mode_one), "inner"))
    mode_two = lax.psum(mode_two, "inner")
    basis_two = orthonormal_rows(mode_two, lax.psum(gram_of(mode_two), "group"))
    along_two = jnp.einsum("ijk,js->isk", flow_field, basis_two, precision=precise)
    levels = jnp.exp2(bit_widths.astype(jnp.float32) - 1.0) - 1.0
    summed_two = lax.psum_scatter(along_two, "group", scatter_dimension=1, tiled=True)
    partial_rows = jnp.einsum("ir,isk->rsk", basis_one, summed_two, precision=precise)
    core_shard = lax.psum_scatter(partial_rows, "inner", scatter_dimension=0, tiled=True)
    peak = lax.pmax(jnp.max(jnp.abs(core_shard)), ("group", "inner"))
    residual_shard = soft_residual(core_shard, peak / levels)
    spread = lax.all_gather(residual_shard, "group", axis=2, tiled=True)
    mixed_core = jnp.einsum(
        "ir,brsk->bisk",
        basis_one,
        lax.all_gather(spread, "inner", axis=1, tiled=True),
        precision=precise,
    )
    error_scale = error_boost * math.sqrt(N1 * N2) / R
    field_error = error_scale * jnp.einsum(
        "bisk,js->bijk", mixed_core, basis_two, precision=precise
    )
    energy_part = jnp.sum(field_error * field_error, axis=2) / N2
    edge_values = bin_edges.astype(jnp.float32)
    ramp_part = jnp.stack(
        [
            jnp.sum(jnp.clip(field_error - edge_values[index_edge] + 0.5, 0.0, 1.0), axis=(2, 3))
            for index_edge in range(NEDGE)
        ],
        axis=-1,
    )
    energy, ramp_sums = lax.psum((energy_part, ramp_part), "group")
    histogram = (ramp_sums[..., :-1] - ramp_sums[..., 1:]) * (NBINS / (N2 * N3))
    return (basis_one, basis_two, core_shard, residual_shard, energy, histogram)


def solution(mesh):
    in_specs = (P("inner", "group", None), P("inner", None), P("group", None), P(), P(), P())
    out_specs = (
        P("inner", None),
        P("group", None),
        P("inner", "group", None),
        P(None, "inner", "group", None),
        P(None, "inner", None),
        P(None, "inner", None),
    )
    return jax.shard_map(local, mesh=mesh, in_specs=in_specs, out_specs=out_specs, check_vma=False)
```

profile of v0, /device:TPU:8, one launch (start us, length us, event | category | flops | bytes accessed | tf_op | source)
XLA Modules:
  0.0 863.6 jit_solution(15359649875850458368)
XLA Ops:
  7.2 0.0 copy-start
  7.2 0.0 copy-start.5
  7.2 0.0 all-reduce.7.cloned.1.call-start
  7.2 0.8 copy-done
  8.0 7.1 multiply_reduce_fusion.2
  15.1 0.1 copy.31
  15.2 26.1 %psum.42 = f32[48,128]{0,1:T(8,128)S(1)} all-reduce(f32[48,128]{0,1:T(8,128)S(1)} %bitcast.98), channel_id=1, replica_groups=mesh['group'=8,'inner'=32] {'group'}, use_global_device_ids=true, to_apply=%region_0.0 | all-reduce | flops 6144 | bytes 49152 | tf_op jit(solution)/shard_map/psum | solution.py:35
  41.3 0.9 fusion.25
  42.2 0.0 copy-done.5
  42.2 2.8 multiply_reduce_fusion.1
  45.0 0.8 copy.39
  45.7 0.0 all-reduce.7.cloned.1.call-update
  45.7 0.0 all-reduce.5.cloned.1.call-start
  45.8 143.9 %all-reduce.7.cloned.1.call-done = (f32[128,128]{0,1:T(8,128)}, f32[192,128]{0,1:T(8,128)}) async-done(((f32[128,128]{0,1:T(8,128)}, f32[192,128]{0,1:T(8,128)}), (f32[128,128]{0,1:T(8,128)}, f32[192,128]{0,1:T(8,128)})) %all-reduce.7.cloned.1.call-update) | async-done | bytes 163856 | tf_op jit(solution)/shard_map/psum | solution.py:36
  189.7 1.9 fusion.26
  191.6 0.0 all-reduce.5.cloned.1.call-update
  191.6 0.2 reduce-scatter.3.cloned.1.call-start
  191.8 64.2 %all-reduce.5.cloned.1.call-done = f32[128,128]{0,1:T(8,128)} async-done(((f32[128,128]{0,1:T(8,128)}), f32[128,128]{0,1:T(8,128)}) %all-reduce.5.cloned.1.call-update) | async-done | bytes 65552 | tf_op jit(solution)/shard_map/psum | solution.py:38
  256.0 0.9 copy.22
  256.9 0.9 fusion.14
  257.8 11.7 %cholesky.55 = f32[128,128]{1,0:T(8,128)S(1)} custom-call(f32[128,128]{1,0:T(8,128)S(1)} %fusion.14), custom_call_target="Cholesky" | custom-call | tf_op jit(solution)/shard_map/jit(cholesky)/cholesky | solution.py:23
  269.5 0.6 compare_reduce_fusion
  270.2 0.7 fusion.11
  270.8 9.8 %custom-call.11 = f32[1,128,128]{1,2,0:T(8,128)S(1)} custom-call(f32[1,128,128]{2,1,0:T(8,128)S(1)} %fusion.11), custom_call_target="InvertDiagBlocksLowerTriangular" | custom-call | tf_op jit(solution)/shard_map/jit(_solve_triangular)/triangular_solve | solution.py:24
  280.6 1.3 fusion.12
  281.9 0.0 copy-start.1
  281.9 0.0 copy-start.6
  281.9 4.8 fusion.6
  286.8 0.0 copy-start.7
  286.8 3.5 copy.57
  290.3 0.0 reduce-scatter.3.cloned.1.call-update
  290.3 0.3 reduce-scatter.5.cloned.1.call-start
  290.6 0.0 copy-done.3
  290.6 0.1 copy.20
  290.7 11.7 %cholesky.44 = f32[128,128]{1,0:T(8,128)S(1)} custom-call(f32[128,128]{1,0:T(8,128)S(1)} %fusion.17), custom_call_target="Cholesky" | custom-call | tf_op jit(solution)/shard_map/jit(cholesky)/cholesky | solution.py:23
  302.5 0.6 compare_reduce_fusion.1
  303.1 0.7 fusion.10
  303.8 9.8 %custom-call.10 = f32[1,128,128]{1,2,0:T(8,128)S(1)} custom-call(f32[1,128,128]{2,1,0:T(8,128)S(1)} %fusion.10), custom_call_target="InvertDiagBlocksLowerTriangular" | custom-call | tf_op jit(solution)/shard_map/jit(_solve_triangular)/triangular_solve | solution.py:24
  313.6 0.3 fusion.15
  313.9 0.0 copy-start.4
  313.9 14.2 %reduce-scatter.3.cloned.1.call-done = f32[48,16,128]{2,0,1:T(8,128)} async-done(((f32[48,128,128]{2,0,1:T(8,128)}), f32[48,16,128]{2,0,1:T(8,128)}) %reduce-scatter.3.cloned.1.call-update) | async-done | bytes 393232 | tf_op jit(solution)/shard_map/reduce_scatter | solution.py:41
  328.1 2.0 fusion.21
  330.1 1.6 copy.23
  331.7 0.0 reduce-scatter.5.cloned.1.call-update
  331.7 0.0 all-gather.2.cloned.1.call-start
  331.8 215.3 %reduce-scatter.5.cloned.1.call-done = f32[4,16,128]{2,1,0:T(8,128)} async-done(((f32[128,16,128]{2,1,0:T(8,128)}), f32[4,16,128]{2,1,0:T(8,128)}) %reduce-scatter.5.cloned.1.call-update) | async-done | bytes 32784 | tf_op jit(solution)/shard_map/reduce_scatter | solution.py:43
  547.1 1.4 broadcast_multiply_fusion.2
  548.5 74.3 %pmax.7 = f32[]{:T(128)} all-reduce(f32[]{:T(128)} %get-tuple-element.34), channel_id=1, replica_groups=mesh['group'=8,'inner'=32] {'group','inner'}, use_global_device_ids=true, to_apply=%region_9.11 | all-reduce | flops 1 | bytes 8 | tf_op jit(solution)/shard_map/pmax | solution.py:44
  622.8 0.0 copy-done.6
  622.8 0.7 add_divide_fusion
  623.5 0.3 fusion.9
  623.8 0.0 copy-start.2
  623.8 14.5 %all_gather.6 = f32[2,4,128,128]{3,2,1,0:T(8,128)} all-gather(f32[2,4,16,128]{3,2,1,0:T(8,128)S(1)} %fusion.9), channel_id=1, replica_groups=mesh['group'=8,'inner'=32] {'group'}, dimensions={2}, use_global_device_ids=true | all-gather | bytes 589824 | tf_op jit(solution)/shard_map/all_gather | solution.py:46
  638.3 0.0 all-gather.2.cloned.1.call-update
  638.3 0.0 copy-done.7
  638.3 0.7 fusion.24
  639.0 135.6 %all-gather.2.cloned.1.call-done = f32[2,128,128,128]{3,2,1,0:T(8,128)} async-done(((f32[2,4,128,128]{3,2,1,0:T(8,128)}), f32[2,128,128,128]{3,2,1,0:T(8,128)}) %all-gather.2.cloned.1.call-update) | async-done | bytes 16777232 | tf_op jit(solution)/shard_map/all_gather | solution.py:50
  774.6 22.9 %fusion = f32[2,128,128,48]{2,3,1,0:T(8,128)S(1)} fusion(f32[2,128,128,128]{3,2,1,0:T(8,128)} %all-gather.2.cloned.1.call-done, f32[128,48]{0,1:T(8,128)S(1)} %fusion.15), kind=kOutput, calls=%fused_computation | convolution fusion | flops 2415919104 | bytes 23093248 | tf_op jit(solution)/shard_map/ir,brsk->bisk/dot_general | solution.py:47
  797.5 0.0 copy-done.4
  797.5 0.0 copy-done.2
  797.5 0.0 copy-done.1
  797.5 32.9 %clamp_reduce_fusion = (f32[2,48]{1,0:T(2,128)S(1)}, f32[2,48]{1,0:T(2,128)S(1)}, f32[2,48]{1,0:T(2,128)S(1)}, f32[2,48]{1,0:T(2,128)S(1)}, f32[2,48]{1,0:T(2,12...) fusion(f32[]{:T(128)} %bitcast.39, f32[]{:T(128)} %bitcast.23, ...), kind=kOutput, calls=%fused_computation.2 | convolution fusion | flops 3715877888 | bytes 6442404 | tf_op jit(solution)/shard_map/bisk,js->bijk/dot_general | solution.py:54
  830.6 25.9 %all-reduce.1 = (f32[2,48,128]{2,1,0:T(8,128)}, f32[2,48,9]{1,0,2:T(2,128)S(1)}) all-reduce(f32[2,48,128]{2,1,0:T(8,128)S(1)} %broadcast_multiply_fusion.1, f32[2,48,9]{1,0,2:T(2,128)S(1)} %constant_dynamic-update-slice_fusion), channel_id=1, replica_groups=mesh['group'=8,'inner'=32] {'group'}, use_global_device_ids=true, to_apply=%region_11.13 | all-reduce | flops 13152 | bytes 105216 | tf_op jit(solution)/shard_map/psum | solution.py:66
  856.5 0.6 copy.24
  (16 shorter events, 0.2 us)
Async XLA Ops:
  7.2 0.8 copy-start
  7.2 35.0 %copy-start.5 = (f32[48,128]{1,0:T(8,128)S(1)}, f32[48,128]{1,0:T(8,128)}, u32[]{:S(2)}) copy-start(f32[48,128]{1,0:T(8,128)} %param.8) | copy-start | bytes 73732
  7.2 182.5 %all-reduce.7.cloned.1.call-start = ((), (), s32[]{:S(2)}) async-start(), calls=%async_computation.6 | async-start | bytes 393216 | tf_op jit(solution)/shard_map/psum | solution.py:36
  45.7 210.2 %all-reduce.5.cloned.1.call-start = ((), (), s32[]{:S(2)}) async-start(), calls=%async_computation.2 | async-start | bytes 131072 | tf_op jit(solution)/shard_map/psum | solution.py:38
  189.7 100.9 %copy-start.3 = (f32[128,128]{0,1:T(8,128)S(1)}, f32[128,128]{0,1:T(8,128)}, u32[]{:S(2)}) copy-start(f32[128,128]{0,1:T(8,128)} %get-tuple-element.29) | copy-start | bytes 196612
  191.6 136.5 %reduce-scatter.3.cloned.1.call-start = ((), (), s32[]{:S(2)}) async-start(), calls=%async_computation.3 | async-start | bytes 3538944 | tf_op jit(solution)/shard_map/reduce_scatter | solution.py:41
  281.9 515.6 %copy-start.1 = (f32[128,192]{0,1:T(8,128)}, f32[128,192]{0,1:T(8,128)S(1)}, u32[]{:S(2)}) copy-start(f32[128,192]{0,1:T(8,128)S(1)} %fusion.12) | copy-start | bytes 294916
  281.9 340.9 %copy-start.6 = (s32[2]{0:T(128)S(1)}, s32[2]{0:T(128)}, u32[]{:S(2)}) copy-start(s32[2]{0:T(128)} %param.11) | copy-start | bytes 28
  286.8 351.5 %copy-start.7 = (s32[9]{0:T(128)S(1)}, s32[9]{0:T(128)}, u32[]{:S(2)}) copy-start(s32[9]{0:T(128)} %param.12) | copy-start | bytes 112
  290.3 256.8 %reduce-scatter.5.cloned.1.call-start = ((), (), s32[]{:S(2)}) async-start(), calls=%async_computation.4 | async-start | bytes 1081344 | tf_op jit(solution)/shard_map/reduce_scatter | solution.py:43
  313.9 483.7 %copy-start.4 = (f32[128,48]{0,1:T(8,128)}, f32[128,48]{0,1:T(8,128)S(1)}, u32[]{:S(2)}) copy-start(f32[128,48]{0,1:T(8,128)S(1)} %fusion.15) | copy-start | bytes 73732
  331.7 442.9 %all-gather.2.cloned.1.call-start = ((), (), s32[]{:S(2)}) async-start(), calls=%async_computation.5 | async-start | bytes 17301504 | tf_op jit(solution)/shard_map/all_gather | solution.py:50
  623.8 173.7 %copy-start.2 = (f32[2,4,16,128]{3,2,1,0:T(8,128)}, f32[2,4,16,128]{3,2,1,0:T(8,128)S(1)}, u32[]{:S(2)}) copy-start(f32[2,4,16,128]{3,2,1,0:T(8,128)S(1)} %fusion.9) | copy-start | bytes 196612
Sparse Core Ops, SparseCore 0:
  45.9 143.7 all-reduce.6
  192.5 63.3 all-reduce.4
  290.4 37.5 reduce-scatter.2
  332.3 214.7 reduce-scatter.4
  638.4 136.1 all-gather.1
where the time goes:
time: 864 us
  waiting for transfers between devices  573 us (66%)
  blocking collectives  141 us (16%)
  matrix products  74.1 us (9%)
  other arithmetic  51.7 us (6%)
  between operations  14 us (2%)
  local copies, waits for them, and re-layouts  9.15 us (1%)
    reduce_scatter x1, waiting for transfers between devices, local(): lax.psum_scatter(partial_rows, 'inner', scatter_dimension=0, tiled=True)  215 us
    psum x1, waiting for transfers between devices, local(): basis_one = orthonormal_rows(mode_one, lax.psum(gram_of(mode_one), 'inner'))  144 us
    all_gather x1, waiting for transfers between devices, local(): lax.all_gather(spread, 'inner', axis=1, tiled=True)  136 us
    pmax x1, blocking collectives, local(): peak = lax.pmax(jnp.max(jnp.abs(core_shard)), ('group', 'inner'))  74.3 us
    psum x1, waiting for transfers between devices, local(): basis_two = orthonormal_rows(mode_two, lax.psum(gram_of(mode_two), 'group'))  64.2 us
    dot_general x1, matrix products, local(): jnp.einsum('bisk,js->bijk', mixed_core, basis_two, precision=precise)  32.9 us
    psum x1, blocking collectives, local(): mode_one = lax.psum(mode_one, 'group')  26.1 us
    psum x1, blocking collectives, local(): energy, ramp_sums = lax.psum((energy_part, ramp_part), 'group')  25.9 us
  transfers between devices with their start and end apart: 5, of which 5 were waited for; matrix products, arithmetic and copies ran while one was open for 3% of the time, Pallas kernels for 0%

commit v1 on v0

--- a/solution.py
+++ b/solution.py
@@ -13,6 +13,10 @@
 precise = lax.Precision.HIGHEST
 two_pi = 2.0 * 3.141592653589793
 error_boost = 16.0
+
+
+def grid_group(frame, along_axis):
+    return jax.lax.all_gather(frame, axis_name=along_axis).sum(axis=0)
 
 
 def gram_of(sketch):
@@ -35,7 +39,7 @@
     mode_one = lax.psum(mode_one, "group")
     basis_one = orthonormal_rows(mode_one, lax.psum(gram_of(mode_one), "inner"))
     mode_two = lax.psum(mode_two, "inner")
-    basis_two = orthonormal_rows(mode_two, lax.psum(gram_of(mode_two), "group"))
+    basis_two = orthonormal_rows(mode_two, grid_group(gram_of(mode_two), "group"))
     along_two = jnp.einsum("ijk,js->isk", flow_field, basis_two, precision=precise)
     levels = jnp.exp2(bit_widths.astype(jnp.float32) - 1.0) - 1.0
     summed_two = lax.psum_scatter(along_two, "group", scatter_dimension=1, tiled=True)

time: 864 us -> 810 us (0.938)
  waiting for transfers between devices: 573 us -> 508 us
  blocking collectives: 141 us -> 154 us
    psum x1 -> x0, waiting for transfers between devices: 64.2 us -> none  [local(): basis_two = orthonormal_rows(mode_two, lax.psum(gram_of(mode_two), 'group'))]
    all_gather x0 -> x1, blocking collectives: none -> 13.6 us  [grid_group(): return jax.lax.all_gather(frame, axis_name=along_axis).sum(axis=0)]
  transfers between devices with their start and end apart: 5 -> 4, of which waited for: 5 -> 4; matrix products, arithmetic and copies ran while one was open for 3% -> 3% of each run, Pallas kernels for 0% -> 0%
where the time goes in v1:
time: 810 us
  waiting for transfers between devices  508 us (63%)
  blocking collectives  154 us (19%)
  matrix products  73.5 us (9%)
  other arithmetic  50.9 us (6%)
  between operations  14 us (2%)
  local copies, waits for them, and re-layouts  8.31 us (1%)
    reduce_scatter x1, waiting for transfers between devices, local(): lax.psum_scatter(partial_rows, 'inner', scatter_dimension=0, tiled=True)  215 us
    psum x1, waiting for transfers between devices, local(): basis_one = orthonormal_rows(mode_one, lax.psum(gram_of(mode_one), 'inner'))  144 us
    all_gather x1, waiting for transfers between devices, local(): lax.all_gather(spread, 'inner', axis=1, tiled=True)  136 us
    pmax x1, blocking collectives, local(): peak = lax.pmax(jnp.max(jnp.abs(core_shard)), ('group', 'inner'))  74.3 us
    dot_general x1, matrix products, local(): jnp.einsum('bisk,js->bijk', mixed_core, basis_two, precision=precise)  32.9 us
    psum x1, blocking collectives, local(): mode_one = lax.psum(mode_one, 'group')  26.1 us
    psum x1, blocking collectives, local(): energy, ramp_sums = lax.psum((energy_part, ramp_part), 'group')  25.9 us
    another operation x6, other arithmetic, orthonormal_rows(): lower_factor = jnp.linalg.cholesky(gram_matrix)  24.8 us
  transfers between devices with their start and end apart: 4, of which 4 were waited for; matrix products, arithmetic and copies ran while one was open for 3% of the time, Pallas kernels for 0%

profile of v1, /device:TPU:8, one launch (start us, length us, event | category | flops | bytes accessed | tf_op | source)
XLA Modules:
  0.0 809.5 jit_solution(15507771966093478503)
XLA Ops:
  7.2 0.0 copy-start
  7.2 0.0 copy-start.5
  7.2 0.0 all-reduce.4.cloned.1.call-start
  7.2 0.8 copy-done
  8.0 7.1 multiply_reduce_fusion.2
  15.1 0.1 copy.29
  15.2 26.1 %psum.35 = f32[48,128]{0,1:T(8,128)S(1)} all-reduce(f32[48,128]{0,1:T(8,128)S(1)} %bitcast.100), channel_id=1, replica_groups=mesh['group'=8,'inner'=32] {'group'}, use_global_device_ids=true, to_apply=%region_0.0 | all-reduce | flops 6144 | bytes 49152 | tf_op jit(solution)/shard_map/psum | solution.py:39
  41.3 0.9 fusion.25
  42.2 0.0 copy-done.5
  42.2 2.8 multiply_reduce_fusion.1
  45.0 0.8 copy.37
  45.7 0.0 all-reduce.4.cloned.1.call-update
  45.7 0.0 reduce-scatter.3.cloned.1.call-start
  45.8 143.9 %all-reduce.4.cloned.1.call-done = (f32[128,128]{0,1:T(8,128)}, f32[192,128]{0,1:T(8,128)}) async-done(((f32[128,128]{0,1:T(8,128)}, f32[192,128]{0,1:T(8,128)}), (f32[128,128]{0,1:T(8,128)}, f32[192,128]{0,1:T(8,128)})) %all-reduce.4.cloned.1.call-update) | async-done | bytes 163856 | tf_op jit(solution)/shard_map/psum | solution.py:40
  189.7 1.3 fusion.26
  190.9 13.6 %all-gather = f32[1024,128]{1,0:T(8,128)S(1)} all-gather(f32[128,128]{1,0:T(8,128)S(1)} %fusion.26), channel_id=2, replica_groups=mesh['group'=8,'inner'=32] {'group'}, dimensions={0}, use_global_device_ids=true | all-gather | bytes 589824 | tf_op jit(solution)/shard_map/all_gather | solution.py:19
  204.5 0.0 copy-start.3
  204.6 0.1 copy.20
  204.7 11.7 %cholesky.55 = f32[128,128]{1,0:T(8,128)S(1)} custom-call(f32[128,128]{1,0:T(8,128)S(1)} %fusion.14), custom_call_target="Cholesky" | custom-call | tf_op jit(solution)/shard_map/jit(cholesky)/cholesky | solution.py:27
  216.4 0.6 compare_reduce_fusion
  217.1 0.7 fusion.11
  217.7 9.8 %custom-call.11 = f32[1,128,128]{1,2,0:T(8,128)S(1)} custom-call(f32[1,128,128]{2,1,0:T(8,128)S(1)} %fusion.11), custom_call_target="InvertDiagBlocksLowerTriangular" | custom-call | tf_op jit(solution)/shard_map/jit(_solve_triangular)/triangular_solve | solution.py:28
  227.5 1.3 fusion.12
  228.8 0.0 copy-start.1
  228.8 0.0 copy-start.6
  228.8 4.8 fusion.6
  233.7 0.0 copy-start.7
  233.7 3.5 copy.54
  237.2 0.0 reduce-scatter.3.cloned.1.call-update
  237.2 0.3 reduce-scatter.5.cloned.1.call-start
  237.5 0.0 copy-done.3
  237.5 0.1 copy.19
  237.6 11.7 %cholesky.44 = f32[128,128]{1,0:T(8,128)S(1)} custom-call(f32[128,128]{1,0:T(8,128)S(1)} %fusion.17), custom_call_target="Cholesky" | custom-call | tf_op jit(solution)/shard_map/jit(cholesky)/cholesky | solution.py:27
  249.4 0.6 compare_reduce_fusion.1
  250.0 0.7 fusion.10
  250.7 9.8 %custom-call.10 = f32[1,128,128]{1,2,0:T(8,128)S(1)} custom-call(f32[1,128,128]{2,1,0:T(8,128)S(1)} %fusion.10), custom_call_target="InvertDiagBlocksLowerTriangular" | custom-call | tf_op jit(solution)/shard_map/jit(_solve_triangular)/triangular_solve | solution.py:28
  260.5 0.3 fusion.15
  260.8 0.0 copy-start.4
  260.8 13.2 %reduce-scatter.3.cloned.1.call-done = f32[48,16,128]{2,0,1:T(8,128)} async-done(((f32[48,128,128]{2,0,1:T(8,128)}), f32[48,16,128]{2,0,1:T(8,128)}) %reduce-scatter.3.cloned.1.call-update) | async-done | bytes 393232 | tf_op jit(solution)/shard_map/reduce_scatter | solution.py:45
  274.0 2.0 fusion.21
  276.0 1.6 copy.21
  277.6 0.0 reduce-scatter.5.cloned.1.call-update
  277.7 0.0 all-gather.3.cloned.1.call-start
  277.7 215.3 %reduce-scatter.5.cloned.1.call-done = f32[4,16,128]{2,1,0:T(8,128)} async-done(((f32[128,16,128]{2,1,0:T(8,128)}), f32[4,16,128]{2,1,0:T(8,128)}) %reduce-scatter.5.cloned.1.call-update) | async-done | bytes 32784 | tf_op jit(solution)/shard_map/reduce_scatter | solution.py:47
  493.0 1.4 broadcast_multiply_fusion.2
  494.4 74.3 %pmax.7 = f32[]{:T(128)} all-reduce(f32[]{:T(128)} %get-tuple-element.34), channel_id=1, replica_groups=mesh['group'=8,'inner'=32] {'group','inner'}, use_global_device_ids=true, to_apply=%region_9.11 | all-reduce | flops 1 | bytes 8 | tf_op jit(solution)/shard_map/pmax | solution.py:48
  568.7 0.0 copy-done.6
  568.7 0.7 add_divide_fusion
  569.3 0.3 fusion.9
  569.6 0.0 copy-start.2
  569.7 14.5 %all_gather.14 = f32[2,4,128,128]{3,2,1,0:T(8,128)} all-gather(f32[2,4,16,128]{3,2,1,0:T(8,128)S(1)} %fusion.9), channel_id=1, replica_groups=mesh['group'=8,'inner'=32] {'group'}, dimensions={2}, use_global_device_ids=true | all-gather | bytes 589824 | tf_op jit(solution)/shard_map/all_gather | solution.py:50
  584.1 0.0 all-gather.3.cloned.1.call-update
  584.1 0.0 copy-done.7
  584.2 0.7 fusion.24
  584.9 135.7 %all-gather.3.cloned.1.call-done = f32[2,128,128,128]{3,2,1,0:T(8,128)} async-done(((f32[2,4,128,128]{3,2,1,0:T(8,128)}), f32[2,128,128,128]{3,2,1,0:T(8,128)}) %all-gather.3.cloned.1.call-update) | async-done | bytes 16777232 | tf_op jit(solution)/shard_map/all_gather | solution.py:54
  720.5 22.9 %fusion = f32[2,128,128,48]{2,3,1,0:T(8,128)S(1)} fusion(f32[2,128,128,128]{3,2,1,0:T(8,128)} %all-gather.3.cloned.1.call-done, f32[128,48]{0,1:T(8,128)S(1)} %fusion.15), kind=kOutput, calls=%fused_computation | convolution fusion | flops 2415919104 | bytes 23093248 | tf_op jit(solution)/shard_map/ir,brsk->bisk/dot_general | solution.py:51
  743.4 0.0 copy-done.4
  743.4 0.0 copy-done.2
  743.4 0.0 copy-done.1
  743.4 32.9 %clamp_reduce_fusion = (f32[2,48]{1,0:T(2,128)S(1)}, f32[2,48]{1,0:T(2,128)S(1)}, f32[2,48]{1,0:T(2,128)S(1)}, f32[2,48]{1,0:T(2,128)S(1)}, f32[2,48]{1,0:T(2,12...) fusion(f32[]{:T(128)} %bitcast.40, f32[]{:T(128)} %bitcast.24, ...), kind=kOutput, calls=%fused_computation.2 | convolution fusion | flops 3715877888 | bytes 6442404 | tf_op jit(solution)/shard_map/bisk,js->bijk/dot_general | solution.py:58
  776.5 25.9 %all-reduce.1 = (f32[2,48,128]{2,1,0:T(8,128)}, f32[2,48,9]{1,0,2:T(2,128)S(1)}) all-reduce(f32[2,48,128]{2,1,0:T(8,128)S(1)} %broadcast_multiply_fusion.1, f32[2,48,9]{1,0,2:T(2,128)S(1)} %constant_dynamic-update-slice_fusion), channel_id=1, replica_groups=mesh['group'=8,'inner'=32] {'group'}, use_global_device_ids=true, to_apply=%region_11.13 | all-reduce | flops 13152 | bytes 105216 | tf_op jit(solution)/shard_map/psum | solution.py:70
  802.4 0.6 copy.22
  (17 shorter events, 0.2 us)
Async XLA Ops:
  7.2 0.8 copy-start
  7.2 35.0 %copy-start.5 = (f32[48,128]{1,0:T(8,128)S(1)}, f32[48,128]{1,0:T(8,128)}, u32[]{:S(2)}) copy-start(f32[48,128]{1,0:T(8,128)} %param.8) | copy-start | bytes 73732
  7.2 182.5 %all-reduce.4.cloned.1.call-start = ((), (), s32[]{:S(2)}) async-start(), calls=%async_computation.5 | async-start | bytes 393216 | tf_op jit(solution)/shard_map/psum | solution.py:40
  45.7 228.3 %reduce-scatter.3.cloned.1.call-start = ((), (), s32[]{:S(2)}) async-start(), calls=%async_computation.2 | async-start | bytes 3538944 | tf_op jit(solution)/shard_map/reduce_scatter | solution.py:45
  204.5 33.0 %copy-start.3 = (f32[128,128]{0,1:T(8,128)S(1)}, f32[128,128]{0,1:T(8,128)}, u32[]{:S(2)}) copy-start(f32[128,128]{0,1:T(8,128)} %get-tuple-element.29) | copy-start | bytes 196612
  228.8 514.6 %copy-start.1 = (f32[128,192]{0,1:T(8,128)}, f32[128,192]{0,1:T(8,128)S(1)}, u32[]{:S(2)}) copy-start(f32[128,192]{0,1:T(8,128)S(1)} %fusion.12) | copy-start | bytes 294916
  228.8 339.8 %copy-start.6 = (s32[2]{0:T(128)S(1)}, s32[2]{0:T(128)}, u32[]{:S(2)}) copy-start(s32[2]{0:T(128)} %param.11) | copy-start | bytes 28
  233.7 350.4 %copy-start.7 = (s32[9]{0:T(128)S(1)}, s32[9]{0:T(128)}, u32[]{:S(2)}) copy-start(s32[9]{0:T(128)} %param.12) | copy-start | bytes 112
  237.2 255.8 %reduce-scatter.5.cloned.1.call-start = ((), (), s32[]{:S(2)}) async-start(), calls=%async_computation.3 | async-start | bytes 1081344 | tf_op jit(solution)/shard_map/reduce_scatter | solution.py:47
  260.8 482.6 %copy-start.4 = (f32[128,48]{0,1:T(8,128)}, f32[128,48]{0,1:T(8,128)S(1)}, u32[]{:S(2)}) copy-start(f32[128,48]{0,1:T(8,128)S(1)} %fusion.15) | copy-start | bytes 73732
  277.7 442.8 %all-gather.3.cloned.1.call-start = ((), (), s32[]{:S(2)}) async-start(), calls=%async_computation.4 | async-start | bytes 17301504 | tf_op jit(solution)/shard_map/all_gather | solution.py:54
  569.6 173.8 %copy-start.2 = (f32[2,4,16,128]{3,2,1,0:T(8,128)}, f32[2,4,16,128]{3,2,1,0:T(8,128)S(1)}, u32[]{:S(2)}) copy-start(f32[2,4,16,128]{3,2,1,0:T(8,128)S(1)} %fusion.9) | copy-start | bytes 196612
Sparse Core Ops, SparseCore 0:
  45.9 143.7 all-reduce.3
  237.3 36.6 reduce-scatter.2
  278.4 214.5 reduce-scatter.4
  584.3 136.2 all-gather.2
